TPU v7x, 512 devices: a whole 4x8x8 slice. The times are simulated.
512 devices in a mesh: dp: 32 (over y, x), feat: 16 (over z, core).
Axes of the slice: x: 4, y: 8, z: 8, core: 2. Of those that a mesh axis runs over, the one named last changes fastest.
Arguments:
- tokens: bfloat16 [4096, 8192], P('dp', 'feat'), may hold values from -6 to 6
- targets: bfloat16 [8192, 8192], P('dp', 'feat'), may hold values from -6 to 6
- first_blocks: bfloat16 [128, 64, 256], P('feat'), may hold values from -0.75 to 0.75
- second_factor_blocks: bfloat16 [128, 256, 256], P('feat'), may hold values from -0.375 to 0.375
- down_blocks: bfloat16 [128, 256, 64], P('feat'), may hold values from -0.375 to 0.375
- first_tangent: bfloat16 [128, 64, 256], P('feat'), may hold values from -0.75 to 0.75
- second_factor_tangent: bfloat16 [128, 256, 256], P('feat'), may hold values from -0.375 to 0.375
- doc_lengths: int32 [32, 32], replicated, may hold values from 1 to 8, as said below
- doc_owners: int32 [32, 32], replicated, may hold values from 0 to 31, as said below
- pack_offsets: int32 [32, 32], replicated, may hold values from 0 to 248, as said below
Outputs:
- hess_first: float32 [128, 64, 256], P('feat', 'dp')
- hess_mixed: float32 [128, 256, 256], P('feat', 'dp')
Inputs may be any that keep to these rules, and one draw needn't show every extreme that they name: `doc_lengths`: the 32 lengths of one loader sum to 128; the longest has exactly 8 rows. `doc_owners`: A loader sends exactly one document to each owner; some owner receives exactly 256 rows in all, and none more. `pack_offsets`: each owner's documents lie end to end from row 0 of its pack, in the order of their loaders.
All inputs are finite; a program needn't handle non-finite values.
Results may differ from a plain program's by a relative error of at most 0.0072.
Values may be sent and summed in bfloat16 or wider, within the bound.
No kernel may reach another device: no remote copies, remote signals or barrier semaphores. Data moves between devices by JAX's collectives and lax.ppermute only.
A program may use at most 64 MiB of HBM per device.

v0:
```python
import jax
import jax.numpy as jnp
from jax import lax
from jax.sharding import PartitionSpec as P

inv_root_two = 0.7071067811865476
inv_root_two_pi = 0.3989422804014327


def curvature(
    tok_rows,
    goal_rows,
    weight,
    first_blocks,
    second_factor_blocks,
    down_blocks,
    first_tangent,
    second_factor_tangent,
):
    features = lax.axis_size("feat")
    row_count = tok_rows.shape[0]
    local_blocks, block_in, block_out = first_blocks.shape
    pair_size = block_out // (local_blocks * features)
    token_blocks = tok_rows.reshape(row_count, local_blocks, block_in)
    goal_blocks = goal_rows.reshape(row_count, local_blocks, block_in)
    split_shape = (local_blocks, block_in, features, local_blocks, pair_size)
    down_shape = (local_blocks, features, local_blocks, pair_size, block_in)
    first_act = jnp.einsum(
        "rki,kiGgc->Ggkcr",
        token_blocks,
        first_blocks.reshape(split_shape),
        preferred_element_type=jnp.float32,
    ).astype(jnp.bfloat16)
    tangents = jnp.einsum(
        "rki,kiGgc->Ggkcr",
        token_blocks,
        first_tangent.reshape(split_shape),
        preferred_element_type=jnp.float32,
    ).astype(jnp.bfloat16)
    out_grad = (
        jnp.einsum(
            "rkd,kGgcd->Ggkcr",
            goal_blocks,
            down_blocks.reshape(down_shape),
            preferred_element_type=jnp.float32,
        )
        * weight
    ).astype(jnp.bfloat16)
    stacked = jnp.stack([first_act, tangents, out_grad], axis=1)
    mixed = lax.all_to_all(stacked, "feat", split_axis=0, concat_axis=3, tiled=True)
    hidden_shape = (local_blocks, block_out, row_count)
    mixed_activation = mixed[0, 0].reshape(hidden_shape)
    mixed_tangent_value = mixed[0, 1].reshape(hidden_shape)
    hidden_grad = mixed[0, 2].reshape(hidden_shape)
    pre_act = jnp.einsum(
        "vca,vcf->vfa", mixed_activation, second_factor_blocks, preferred_element_type=jnp.float32
    )
    pre_tan = jnp.einsum(
        "vca,vcf->vfa",
        mixed_tangent_value,
        second_factor_blocks,
        preferred_element_type=jnp.float32,
    ) + jnp.einsum(
        "vca,vcf->vfa", mixed_activation, second_factor_tangent, preferred_element_type=jnp.float32
    )
    density = jnp.exp(-0.5 * pre_act * pre_act) * inv_root_two_pi
    normal_cdf = 0.5 * (1.0 + lax.erf(pre_act * inv_root_two))
    preactivation_gradient = (hidden_grad * (normal_cdf + pre_act * density)).astype(jnp.bfloat16)
    preactivation_tangent_gradient = (
        hidden_grad * (density * (2.0 - pre_act * pre_act)) * pre_tan
    ).astype(jnp.bfloat16)
    hess_mixed = jnp.einsum(
        "evp,eqp->evq",
        mixed_tangent_value,
        preactivation_gradient,
        preferred_element_type=jnp.float32,
    ) + jnp.einsum(
        "evp,eqp->evq",
        mixed_activation,
        preactivation_tangent_gradient,
        preferred_element_type=jnp.float32,
    )
    back_mixed = jnp.einsum(
        "bip,bfi->bfp",
        preactivation_tangent_gradient,
        second_factor_blocks,
        preferred_element_type=jnp.float32,
    ) + jnp.einsum(
        "bip,bfi->bfp",
        preactivation_gradient,
        second_factor_tangent,
        preferred_element_type=jnp.float32,
    )
    back_split = back_mixed.astype(jnp.bfloat16).reshape(
        local_blocks, features, local_blocks, pair_size, row_count
    )
    back_first = lax.all_to_all(back_split, "feat", split_axis=1, concat_axis=0, tiled=True)
    back_first = back_first.reshape(local_blocks * features, local_blocks, pair_size, row_count)
    hess_first = jnp.einsum(
        "gkcr,rki->kigc", back_first, token_blocks, preferred_element_type=jnp.float32
    ).reshape(local_blocks, block_in, block_out)
    return (hess_first, hess_mixed)


def per_device(
    tokens,
    targets,
    first_blocks,
    second_factor_blocks,
    down_blocks,
    first_tangent,
    second_factor_tangent,
    doc_lengths,
    doc_owners,
    pack_offsets,
):
    loaders = lax.axis_size("dp")
    device = lax.axis_index("dp")
    tok_count = tokens.shape[0]
    feature_cols = tokens.shape[1]
    slot_rows = 2 * tok_count // loaders
    position = jnp.arange(slot_rows, dtype=jnp.int32)
    mine = (doc_owners == device).astype(jnp.int32)
    first_row = jnp.sum(mine * pack_offsets, axis=1)
    doc_span = jnp.sum(mine * doc_lengths, axis=1)
    in_slot = position[None, :] < doc_span[:, None]
    source = jnp.where(in_slot, first_row[:, None] + position[None, :], 0)
    outgoing = jnp.take(targets, source.reshape(-1), axis=0).reshape(
        loaders, slot_rows, feature_cols
    )
    arrived = lax.all_to_all(outgoing, "dp", split_axis=0, concat_axis=0, tiled=True)
    my_lengths = lax.dynamic_index_in_dim(doc_lengths, device, 0, keepdims=False)
    my_owners = lax.dynamic_index_in_dim(doc_owners, device, 0, keepdims=False)
    my_starts = jnp.cumsum(my_lengths) - my_lengths
    token_pos = jnp.arange(tok_count, dtype=jnp.int32)
    inside = (token_pos[:, None] >= my_starts[None, :]) & (
        token_pos[:, None] < (my_starts + my_lengths)[None, :]
    )
    inside_int = inside.astype(jnp.int32)
    goal_index = (
        jnp.sum(inside_int * (my_owners * slot_rows - my_starts)[None, :], axis=1) + token_pos
    )
    weight = jnp.sum(inside.astype(jnp.float32) / my_lengths.astype(jnp.float32)[None, :], axis=1)
    goal_rows = jnp.take(arrived.reshape(loaders * slot_rows, feature_cols), goal_index, axis=0)
    hess_first, hess_mixed = curvature(
        tokens,
        goal_rows,
        weight,
        first_blocks,
        second_factor_blocks,
        down_blocks,
        first_tangent,
        second_factor_tangent,
    )
    local_blocks = hess_first.shape[0]
    first_part = hess_first.reshape(local_blocks, loaders, -1)
    mixed_part = hess_mixed.reshape(local_blocks, loaders, -1)
    first_width = first_part.shape[2]
    partials = jnp.concatenate([first_part, mixed_part], axis=2)
    gathered = lax.all_to_all(partials, "dp", split_axis=1, concat_axis=1, tiled=True)
    total = jnp.sum(gathered, axis=1)
    hess_first = total[:, :first_width].reshape(local_blocks, -1, hess_first.shape[2])
    hess_mixed = total[:, first_width:].reshape(local_blocks, -1, hess_mixed.shape[2])
    return (hess_first, hess_mixed)


def solution(mesh):
    in_specs = (
        P("dp", "feat"),
        P("dp", "feat"),
        P("feat", None, None),
        P("feat", None, None),
        P("feat", None, None),
        P("feat", None, None),
        P("feat", None, None),
        P(),
        P(),
        P(),
    )
    out_specs = (P("feat", "dp", None), P("feat", "dp", None))
    return jax.shard_map(
        per_device, mesh=mesh, in_specs=in_specs, out_specs=out_specs, check_vma=False
    )
```

profile of v0, /device:TPU:1, one launch (start us, length us, event | category | flops | bytes accessed | tf_op | source)
XLA Modules:
  0.0 198.2 jit_solution(6791670290175771214)
XLA Ops:
  0.7 1.0 select_reduce_fusion.1
  2.0 2.3 %gather_fusion = bf16[256,512]{1,0:T(8,128)(2,1)S(1)} fusion(bf16[256,512]{1,0:T(8,128)(2,1)} %param.11, s32[1024]{0:T(1024)S(1)} %pad_clamp_fusion.1), kind=kCustom, calls=%fused_computation | custom fusion | bytes 525312 | tf_op jit(solution)/shard_map/jit(_take)/gather | solution.py:128
  4.2 0.8 bitcast_select_fusion
  5.0 10.5 %all-to-all-start = ((bf16[32,8,512]{2,1,0:T(8,128)(2,1)}), bf16[32,8,512]{2,1,0:T(8,128)(2,1)S(1)}, u32[]{:S(2)}, u32[]{:S(2)}) async-start(bf16[32,8,512]{2,1,0:T(8,128)(2,1)} %bitcast_select_fusion), calls=%async_computation | async-start | bytes 524288 | tf_op jit(solution)/shard_map/all_to_all | solution.py:131
  17.9 1.1 copy.89
  19.9 7.0 %all-to-all-done = bf16[32,8,512]{2,1,0:T(8,128)(2,1)S(1)} async-done(((bf16[32,8,512]{2,1,0:T(8,128)(2,1)}), bf16[32,8,512]{2,1,0:T(8,128)(2,1)S(1)}, u32[]{:S(2)}, u32[]{:S(2)}) %all-to-all-start) | async-done | bytes 262176 | tf_op jit(solution)/shard_map/all_to_all | solution.py:131
  26.8 0.8 gather_fusion.1
  27.8 1.3 fusion.5
  29.8 52.3 %all_to_all.43 = bf16[16,3,8,8,2,128]{5,2,4,3,1,0:T(8,128)(2,1)S(1)} all-to-all(bf16[16,3,8,8,2,128]{5,2,4,3,1,0:T(8,128)(2,1)S(1)} %copy.92), channel_id=1, replica_groups=mesh['dp'=32,'feat'=16] {'feat'}, dimensions={0} | all-to-all | bytes 3145728 | tf_op jit(solution)/shard_map/all_to_all | solution.py:50
  83.3 1.6 copy.94
  84.9 1.6 copy.97
  86.9 0.9 fusion.16
  88.7 0.8 copy-done.3
  90.5 1.1 copy.102
  91.6 4.3 %all-to-all-start.2 = ((bf16[8,16,8,2,128]{4,0,3,2,1:T(8,128)(2,1)}), bf16[8,16,8,2,128]{4,0,3,2,1:T(8,128)(2,1)}, u32[]{:S(2)}, u32[]{:S(2)}) async-start(bf16[8,16,8,2,128]{4,0,3,2,1:T(8,128)(2,1)} %bitcast.37), calls=%async_computation.2 | async-start | bytes 1048576 | tf_op jit(solution)/shard_map/all_to_all | solution.py:97
  97.6 1.5 reshape.162
  99.1 2.8 %copy.110 = f32[8,32,2048]{2,0,1:T(8,128)S(1)} copy(f32[8,32,2048]{2,1,0:T(8,128)} %reshape.162) | data formatting | bytes 4194304 | tf_op jit(solution)/shard_map/reshape | solution.py:157
  101.9 9.7 %all-to-all-done.2 = bf16[8,16,8,2,128]{4,0,3,2,1:T(8,128)(2,1)} async-done(((bf16[8,16,8,2,128]{4,0,3,2,1:T(8,128)(2,1)}), bf16[8,16,8,2,128]{4,0,3,2,1:T(8,128)(2,1)}, u32[]{:S(2)}, u32[]{:S(2)}) %all-to-all-start.2) | async-done | bytes 524320 | tf_op jit(solution)/shard_map/all_to_all | solution.py:97
  111.6 2.2 %convolution_bitcast_fusion.1 = f32[8,64,128,2]{2,1,3,0:T(8,128)} fusion(bf16[128,8,64,1]{0,2,3,1:T(8,128)(2,1)S(1)} %bitcast.114, bf16[8,16,8,2,128]{4,0,3,2,1:T(8,128)(2,1)} %all-to-all-done.2), kind=kOutput, calls=%fused_computation.22 | convolution fusion | flops 33554432 | bytes 1179648 | tf_op jit(solution)/shard_map/gkcr,rki->kigc/dot_general | solution.py:99
  113.8 7.1 %copy.104 = f32[8,64,128,2]{0,3,2,1:T(2,128)} copy(f32[8,64,128,2]{2,1,3,0:T(8,128)} %convolution_bitcast_fusion.1) | data formatting | bytes 1048576 | tf_op jit(solution)/shard_map/gkcr,rki->kigc/dot_general | solution.py:99
  120.9 5.8 %copy.109 = f32[8,32,512]{2,0,1:T(8,128)} copy(f32[8,32,512]{0,2,1:T(8,128)} %bitcast.103) | data formatting | bytes 1048576 | tf_op jit(solution)/shard_map/reshape;reshape | solution.py:156
  126.7 1.2 pad_maximum_fusion
  128.0 67.1 %all_to_all.44 = f32[8,32,2560]{2,0,1:T(8,128)} all-to-all(f32[8,32,2560]{2,0,1:T(8,128)S(1)} %pad_maximum_fusion), channel_id=1, replica_groups=mesh['dp'=32,'feat'=16] {'dp'}, dimensions={1} | all-to-all | bytes 5242880 | tf_op jit(solution)/shard_map/all_to_all | solution.py:160
  195.1 1.9 reduce_sum.52
  (60 shorter events, 10.6 us)
Async XLA Ops:
  0.6 85.9 %copy-start = (bf16[8,256,256]{2,1,0:T(8,128)(2,1)S(1)}, bf16[8,256,256]{2,1,0:T(8,128)(2,1)}, u32[]{:S(2)}) copy-start(bf16[8,256,256]{2,1,0:T(8,128)(2,1)} %param.13) | copy-start | bytes 3145732
  0.6 16.8 %copy-start.11 = (bf16[128,512]{1,0:T(8,128)(2,1)S(1)}, bf16[128,512]{1,0:T(8,128)(2,1)}, u32[]{:S(2)}) copy-start(bf16[128,512]{1,0:T(8,128)(2,1)} %param.10) | copy-start | bytes 393220
  0.7 16.9 %copy-start.8 = (bf16[8,64,256]{2,1,0:T(8,128)(2,1)S(1)}, bf16[8,64,256]{2,1,0:T(8,128)(2,1)}, u32[]{:S(2)}) copy-start(bf16[8,64,256]{2,1,0:T(8,128)(2,1)} %param.12) | copy-start | bytes 786436
  1.9 15.9 %copy-start.9 = (bf16[8,256,64]{1,2,0:T(8,128)(2,1)S(1)}, bf16[8,256,64]{1,2,0:T(8,128)(2,1)}, u32[]{:S(2)}) copy-start(bf16[8,256,64]{1,2,0:T(8,128)(2,1)} %param.14) | copy-start | bytes 786436
  1.9 17.0 %copy-start.10 = (bf16[8,64,256]{2,1,0:T(8,128)(2,1)S(1)}, bf16[8,64,256]{2,1,0:T(8,128)(2,1)}, u32[]{:S(2)}) copy-start(bf16[8,64,256]{2,1,0:T(8,128)(2,1)} %param.15) | copy-start | bytes 786436
  5.0 21.8 %all-to-all-start = ((bf16[32,8,512]{2,1,0:T(8,128)(2,1)}), bf16[32,8,512]{2,1,0:T(8,128)(2,1)S(1)}, u32[]{:S(2)}, u32[]{:S(2)}) async-start(bf16[32,8,512]{2,1,0:T(8,128)(2,1)} %bitcast_select_fusion), calls=%async_computation | async-start | bytes 524288 | tf_op jit(solution)/shard_map/all_to_all | solution.py:131
  83.3 4.5 %copy-start.1 = (bf16[1,1,8,128,2,128]{5,2,4,3,1,0:T(8,128)(2,1)}, bf16[1,1,8,128,2,128]{5,2,4,3,1,0:T(8,128)(2,1)S(1)}, u32[]{:S(2)}) copy-start(bf16[1,1,8,128,2,128]{5,2,4,3,1,0:T(8,128)(2,1)S(1)} %copy.95) | copy-start | bytes 1572868
  86.9 1.2 copy-start.7
  87.8 2.2 %copy-start.5 = (bf16[8,256,128]{1,2,0:T(8,128)(2,1)}, bf16[8,256,128]{1,2,0:T(8,128)(2,1)S(1)}, u32[]{:S(2)}) copy-start(bf16[8,256,128]{1,2,0:T(8,128)(2,1)S(1)} %get-tuple-element.10) | copy-start | bytes 1572868
  88.7 0.8 copy-start.3
  90.5 5.4 %copy-start.6 = (bf16[8,256,128]{1,2,0:T(8,128)(2,1)S(1)}, bf16[8,256,128]{1,2,0:T(8,128)(2,1)}, u32[]{:S(2)}) copy-start(bf16[8,256,128]{1,2,0:T(8,128)(2,1)} %copy-done.5) | copy-start | bytes 1572868
  91.6 20.0 %all-to-all-start.2 = ((bf16[8,16,8,2,128]{4,0,3,2,1:T(8,128)(2,1)}), bf16[8,16,8,2,128]{4,0,3,2,1:T(8,128)(2,1)}, u32[]{:S(2)}, u32[]{:S(2)}) async-start(bf16[8,16,8,2,128]{4,0,3,2,1:T(8,128)(2,1)} %bitcast.37), calls=%async_computation.2 | async-start | bytes 1048576 | tf_op jit(solution)/shard_map/all_to_all | solution.py:97
  95.9 1.0 copy-start.2
  96.0 1.2 copy-start.4
where the time goes:
time: 199 us; the launch traced here: 198 us
  blocking collectives  119 us (60%)
  local copies, waits for them, and re-layouts  32.2 us (16%)
  waiting for transfers between devices  16.6 us (8%)
  starting transfers between devices  14.8 us (7%)
  matrix products  7.74 us (4%)
  other arithmetic  6.5 us (3%)
    all_to_all x1, blocking collectives, per_device(): lax.all_to_all(partials, 'dp', split_axis=1, concat_axis=1, tiled=True)  67.1 us
    all_to_all x1, blocking collectives, curvature(): lax.all_to_all(stacked, 'feat', split_axis=0, concat_axis=3, tiled=True)  52.3 us
    all_to_all x1, starting transfers between devices, per_device(): lax.all_to_all(outgoing, 'dp', split_axis=0, concat_axis=0, tiled=True)  10.5 us
    all_to_all x1, waiting for transfers between devices, curvature(): lax.all_to_all(back_split, 'feat', split_axis=1, concat_axis=0, tiled=True)  9.69 us
    dot_general x1, local copies, waits for them, and re-layouts, curvature(): jnp.einsum('gkcr,rki->kigc', back_first, token_blocks, preferred_element_...  7.09 us
    all_to_all x1, waiting for transfers between devices, per_device(): lax.all_to_all(outgoing, 'dp', split_axis=0, concat_axis=0, tiled=True)  6.95 us
    another operation x1, local copies, waits for them, and re-layouts, per_device(): first_part = hess_first.reshape(local_blocks, loaders, -1)  5.85 us
    unnamed x29, local copies, waits for them, and re-layouts  4.36 us
  transfers between devices with their start and end apart: 2, of which 2 were waited for; matrix products, arithmetic and copies ran while one was open for 5% of the time, Pallas kernels for 0%

commit v1 on v0

--- a/solution.py
+++ b/solution.py
@@ -157,7 +157,17 @@
     mixed_part = hess_mixed.reshape(local_blocks, loaders, -1)
     first_width = first_part.shape[2]
     partials = jnp.concatenate([first_part, mixed_part], axis=2)
-    gathered = lax.all_to_all(partials, "dp", split_axis=1, concat_axis=1, tiled=True)
+
+    def turn_skins(d0, dimension_no, xin):
+        r_now = jnp.concatenate(
+            jax.lax.all_to_all(
+                jnp.stack(jnp.split(xin, jax.lax.axis_size("dp"), axis=d0)), "dp", 0, 0
+            ),
+            axis=dimension_no,
+        )
+        return r_now
+
+    gathered = turn_skins(1, dimension_no=1, xin=partials)
     total = jnp.sum(gathered, axis=1)
     hess_first = total[:, :first_width].reshape(local_blocks, -1, hess_first.shape[2])
     hess_mixed = total[:, first_width:].reshape(local_blocks, -1, hess_mixed.shape[2])

time: 199 us -> 203 us (1.020)
  local copies, waits for them, and re-layouts: 32.2 us -> 28.1 us
  other arithmetic: 6.5 us -> 10.3 us
  matrix products: 7.74 us -> 10.2 us
    unnamed x0 -> x31, other arithmetic: none -> 3.39 us
    reshape x2 -> x1, local copies, waits for them, and re-layouts: 4.34 us -> 1.71 us  [per_device(): mixed_part = hess_mixed.reshape(local_blocks, loaders, -1)]
    unnamed x29 -> x25, local copies, waits for them, and re-layouts: 4.36 us -> 2.88 us
where the time goes in v1:
time: 203 us; the launch traced here: 201 us
  blocking collectives  119 us (59%)
  local copies, waits for them, and re-layouts  28.1 us (14%)
  waiting for transfers between devices  17.6 us (9%)
  starting transfers between devices  14.8 us (7%)
  other arithmetic  10.3 us (5%)
  matrix products  10.2 us (5%)
    all_to_all x1, blocking collectives, turn_skins(): jax.lax.all_to_all(jnp.stack(jnp.split(xin, jax.lax.axis_size('dp'), axis...  67 us
    all_to_all x1, blocking collectives, curvature(): lax.all_to_all(stacked, 'feat', split_axis=0, concat_axis=3, tiled=True)  52.3 us
    all_to_all x1, waiting for transfers between devices, curvature(): lax.all_to_all(back_split, 'feat', split_axis=1, concat_axis=0, tiled=True)  10.7 us
    all_to_all x1, starting transfers between devices, per_device(): lax.all_to_all(outgoing, 'dp', split_axis=0, concat_axis=0, tiled=True)  10.5 us
    dot_general x1, local copies, waits for them, and re-layouts, curvature(): jnp.einsum('gkcr,rki->kigc', back_first, token_blocks, preferred_element_...  7.09 us
    all_to_all x1, waiting for transfers between devices, per_device(): lax.all_to_all(outgoing, 'dp', split_axis=0, concat_axis=0, tiled=True)  6.94 us
    another operation x1, local copies, waits for them, and re-layouts, per_device(): first_part = hess_first.reshape(local_blocks, loaders, -1)  5.87 us
    all_to_all x1, starting transfers between devices, curvature(): lax.all_to_all(back_split, 'feat', split_axis=1, concat_axis=0, tiled=True)  4.32 us
  transfers between devices with their start and end apart: 2, of which 2 were waited for; matrix products, arithmetic and copies ran while one was open for 5% of the time, Pallas kernels for 0%

profile of v1, /device:TPU:1, one launch (start us, length us, event | category | flops | bytes accessed | tf_op | source)
XLA Modules:
  0.0 201.5 jit_solution(17625875082988256325)
XLA Ops:
  0.7 1.0 select_reduce_fusion.1
  2.0 2.2 %gather_fusion = bf16[256,512]{1,0:T(8,128)(2,1)S(1)} fusion(bf16[256,512]{1,0:T(8,128)(2,1)} %param.11, s32[1024]{0:T(1024)S(1)} %pad_clamp_fusion.1), kind=kCustom, calls=%fused_computation | custom fusion | bytes 525312 | tf_op jit(solution)/shard_map/jit(_take)/gather | solution.py:128
  4.2 0.8 bitcast_select_fusion
  5.0 10.5 %all-to-all-start = ((bf16[32,8,512]{2,1,0:T(8,128)(2,1)}), bf16[32,8,512]{2,1,0:T(8,128)(2,1)S(1)}, u32[]{:S(2)}, u32[]{:S(2)}) async-start(bf16[32,8,512]{2,1,0:T(8,128)(2,1)} %bitcast_select_fusion), calls=%async_computation | async-start | bytes 524288 | tf_op jit(solution)/shard_map/all_to_all | solution.py:131
  17.9 1.1 copy.88
  19.9 6.9 %all-to-all-done = bf16[32,8,512]{2,1,0:T(8,128)(2,1)S(1)} async-done(((bf16[32,8,512]{2,1,0:T(8,128)(2,1)}), bf16[32,8,512]{2,1,0:T(8,128)(2,1)S(1)}, u32[]{:S(2)}, u32[]{:S(2)}) %all-to-all-start) | async-done | bytes 262176 | tf_op jit(solution)/shard_map/all_to_all | solution.py:131
  26.8 0.8 gather_fusion.1
  27.8 1.3 fusion.5
  29.8 52.3 %all_to_all.43 = bf16[16,3,8,8,2,128]{5,2,4,3,1,0:T(8,128)(2,1)S(1)} all-to-all(bf16[16,3,8,8,2,128]{5,2,4,3,1,0:T(8,128)(2,1)S(1)} %copy.91), channel_id=1, replica_groups=mesh['dp'=32,'feat'=16] {'feat'}, dimensions={0} | all-to-all | bytes 3145728 | tf_op jit(solution)/shard_map/all_to_all | solution.py:50
  83.3 1.6 copy.93
  84.9 1.6 copy.96
  86.9 0.9 fusion.16
  89.7 1.1 copy.101
  90.8 4.3 %all-to-all-start.2 = ((bf16[8,16,8,2,128]{4,0,3,2,1:T(8,128)(2,1)}), bf16[8,16,8,2,128]{4,0,3,2,1:T(8,128)(2,1)}, u32[]{:S(2)}, u32[]{:S(2)}) async-start(bf16[8,16,8,2,128]{4,0,3,2,1:T(8,128)(2,1)} %bitcast.37), calls=%async_computation.2 | async-start | bytes 1048576 | tf_op jit(solution)/shard_map/all_to_all | solution.py:97
  95.1 1.5 fusion.24
  96.6 1.8 convolution_add_fusion
  98.4 1.7 reshape.164
  100.1 10.7 %all-to-all-done.2 = bf16[8,16,8,2,128]{4,0,3,2,1:T(8,128)(2,1)} async-done(((bf16[8,16,8,2,128]{4,0,3,2,1:T(8,128)(2,1)}), bf16[8,16,8,2,128]{4,0,3,2,1:T(8,128)(2,1)}, u32[]{:S(2)}, u32[]{:S(2)}) %all-to-all-start.2) | async-done | bytes 524320 | tf_op jit(solution)/shard_map/all_to_all | solution.py:97
  110.8 2.2 %convolution_bitcast_fusion.1 = f32[8,64,128,2]{2,1,3,0:T(8,128)} fusion(bf16[128,8,64,1]{0,2,3,1:T(8,128)(2,1)S(1)} %bitcast.180, bf16[8,16,8,2,128]{4,0,3,2,1:T(8,128)(2,1)} %all-to-all-done.2), kind=kOutput, calls=%fused_computation.83 | convolution fusion | flops 33554432 | bytes 1179648 | tf_op jit(solution)/shard_map/gkcr,rki->kigc/dot_general | solution.py:99
  113.0 7.1 %copy.103 = f32[8,64,128,2]{0,3,2,1:T(2,128)} copy(f32[8,64,128,2]{2,1,3,0:T(8,128)} %convolution_bitcast_fusion.1) | data formatting | bytes 1048576 | tf_op jit(solution)/shard_map/gkcr,rki->kigc/dot_general | solution.py:99
  120.1 5.9 %copy.108 = f32[8,32,512]{2,1,0:T(8,128)} copy(f32[8,32,512]{0,2,1:T(8,128)} %bitcast.169) | data formatting | bytes 1048576 | tf_op jit(solution)/shard_map/reshape;reshape | solution.py:156
  126.0 1.0 bitcast_dynamic-update-slice_fusion.30
  129.7 67.0 %all_to_all.44 = f32[32,8,1,2560]{3,2,1,0:T(1,128)} all-to-all(f32[32,8,1,2560]{3,2,1,0:T(1,128)S(1)} %fusion.64), channel_id=1, replica_groups=mesh['dp'=32,'feat'=16] {'dp'}, dimensions={0} | all-to-all | bytes 5242880 | tf_op jit(solution)/shard_map/all_to_all | solution.py:163
  196.7 3.4 %reduce_sum.52 = f32[8,2560]{1,0:T(8,128)S(1)} reduce(f32[32,8,1,2560]{3,2,1,0:T(1,128)} %all_to_all.44, f32[]{:T(128)} %constant.57.clone.1), dimensions={0,2}, to_apply=%region_5.6 | reduce | flops 634880 | bytes 2703364 | tf_op jit(solution)/shard_map/reduce_sum | solution.py:171
  (86 shorter events, 11.5 us)
Async XLA Ops:
  0.6 85.9 %copy-start = (bf16[8,256,256]{2,1,0:T(8,128)(2,1)S(1)}, bf16[8,256,256]{2,1,0:T(8,128)(2,1)}, u32[]{:S(2)}) copy-start(bf16[8,256,256]{2,1,0:T(8,128)(2,1)} %param.13) | copy-start | bytes 3145732
  0.6 16.8 %copy-start.9 = (bf16[128,512]{1,0:T(8,128)(2,1)S(1)}, bf16[128,512]{1,0:T(8,128)(2,1)}, u32[]{:S(2)}) copy-start(bf16[128,512]{1,0:T(8,128)(2,1)} %param.10) | copy-start | bytes 393220
  0.7 16.9 %copy-start.6 = (bf16[8,64,256]{2,1,0:T(8,128)(2,1)S(1)}, bf16[8,64,256]{2,1,0:T(8,128)(2,1)}, u32[]{:S(2)}) copy-start(bf16[8,64,256]{2,1,0:T(8,128)(2,1)} %param.12) | copy-start | bytes 786436
  0.7 17.2 %copy-start.7 = (bf16[8,256,64]{1,2,0:T(8,128)(2,1)S(1)}, bf16[8,256,64]{1,2,0:T(8,128)(2,1)}, u32[]{:S(2)}) copy-start(bf16[8,256,64]{1,2,0:T(8,128)(2,1)} %param.14) | copy-start | bytes 786436
  2.0 17.0 %copy-start.8 = (bf16[8,64,256]{2,1,0:T(8,128)(2,1)S(1)}, bf16[8,64,256]{2,1,0:T(8,128)(2,1)}, u32[]{:S(2)}) copy-start(bf16[8,64,256]{2,1,0:T(8,128)(2,1)} %param.15) | copy-start | bytes 786436
  5.0 21.8 %all-to-all-start = ((bf16[32,8,512]{2,1,0:T(8,128)(2,1)}), bf16[32,8,512]{2,1,0:T(8,128)(2,1)S(1)}, u32[]{:S(2)}, u32[]{:S(2)}) async-start(bf16[32,8,512]{2,1,0:T(8,128)(2,1)} %bitcast_select_fusion), calls=%async_computation | async-start | bytes 524288 | tf_op jit(solution)/shard_map/all_to_all | solution.py:131
  83.0 3.5 %copy-start.2 = (bf16[1,1,8,128,2,128]{5,2,4,3,1,0:T(8,128)(2,1)}, bf16[1,1,8,128,2,128]{5,2,4,3,1,0:T(8,128)(2,1)S(1)}, u32[]{:S(2)}) copy-start(bf16[1,1,8,128,2,128]{5,2,4,3,1,0:T(8,128)(2,1)S(1)} %copy.97) | copy-start | bytes 1572868
  86.9 1.2 copy-start.5
  87.8 1.4 copy-start.4
  89.2 5.9 %copy-start.3 = (bf16[1,1,8,128,2,128]{5,2,4,3,1,0:T(8,128)(2,1)S(1)}, bf16[1,1,8,128,2,128]{5,2,4,3,1,0:T(8,128)(2,1)}, u32[]{:S(2)}) copy-start(bf16[1,1,8,128,2,128]{5,2,4,3,1,0:T(8,128)(2,1)} %copy-done.2) | copy-start | bytes 1572868
  90.8 20.0 %all-to-all-start.2 = ((bf16[8,16,8,2,128]{4,0,3,2,1:T(8,128)(2,1)}), bf16[8,16,8,2,128]{4,0,3,2,1:T(8,128)(2,1)}, u32[]{:S(2)}, u32[]{:S(2)}) async-start(bf16[8,16,8,2,128]{4,0,3,2,1:T(8,128)(2,1)} %bitcast.37), calls=%async_computation.2 | async-start | bytes 1048576 | tf_op jit(solution)/shard_map/all_to_all | solution.py:97
  126.0 1.1 copy-start.1
